TPU v7x, 32 devices: a whole 2x2x4 slice. The times are simulated.
32 devices in a mesh: snp: 8 (over z, y), ind: 4 (over x, core).
Axes of the slice: x: 2, y: 2, z: 4, core: 2. Of those that a mesh axis runs over, the one named last changes fastest.
Arguments:
- beta_hat: float32 [64, 8192], P('ind', 'snp'), may hold values from -8 to 8
- ld_band: float32 [8192, 1024], P('snp'), as said below
- band_start: int32 [64], P('snp'), may hold values from -480 to 7648, as said below
- heritability: float32 [64], P('ind'), may hold values from 0.2 to 0.6
- genotypes: bfloat16 [4096, 8192], P('ind', 'snp'), may hold values from 0 to 2, as said below
Outputs:
- weights: float32 [64, 8192], P('ind', 'snp')
- scores: float32 [64, 4096], P(None, ('ind', 'snp'))
Inputs may be any that keep to these rules, and one draw needn't show every extreme that they name: ld_band is a symmetric matrix R in band form: entry k of row i is R[i, band_start[i // 128] + k]; R[i, i] = 1; R[i, j] = 0 when |i - j| > 416 or j lies outside the SNPs; the off-diagonal magnitudes of a row sum to 2.5 at most. `band_start`: block b's window starts at 128 * b - 416 - k with k from 0 to 64; the first block has k = 64 and the last block k = 0. `genotypes`: dosages are 0, 1 or 2.
All inputs are finite; a program needn't handle non-finite values.
Results may differ from a plain program's by a relative error of at most 0.0021.
Values may be sent and summed in bfloat16 or wider, within the bound.
No kernel may reach another device: no remote copies, remote signals or barrier semaphores. Data moves between devices by JAX's collectives and lax.ppermute only.
A program may use at most 64 MiB of HBM per device.

v0:
```python
import jax
import jax.numpy as jnp
from jax import lax
from jax.sharding import PartitionSpec as P

BLK = 128
ITERS = 2
M_GENOME = 1100000
N_GWAS = 1000000


def padded_2(block, sides, width):
    for axis, dim in sides:
        count = lax.axis_size(axis)
        forward = [(i, i + 1) for i in range(count - 1)]
        backward = [(target, source) for source, target in forward]
        low = lax.ppermute(
            lax.slice_in_dim(block, block.shape[dim] - width, None, axis=dim), axis, forward
        )
        high = lax.ppermute(lax.slice_in_dim(block, 0, width, axis=dim), axis, backward)
        block = jnp.concatenate([low, block, high], axis=dim)
    return block


def apply_operator(vector, ld_band, band_start, ridge_shift):
    band_cols = ld_band.shape[1]
    halo_cols = band_cols - BLK
    padded = padded_2(vector, (("snp", 1),), halo_cols)
    local_rows = vector.shape[1]
    offsets = band_start - lax.axis_index("snp") * local_rows + halo_cols
    windows = jax.vmap(lambda row_begin: lax.dynamic_slice_in_dim(padded, row_begin, band_cols, 1))(
        offsets
    )
    blocks = ld_band.reshape(band_start.shape[0], BLK, band_cols)
    product = jnp.einsum("btk,brk->tbr", windows, blocks, precision=lax.Precision.HIGHEST)
    return product.reshape(vector.shape) + ridge_shift[:, None] * vector


def paired_sums(residual, product):
    return lax.psum(
        (jnp.sum(residual * residual, axis=1), jnp.sum(residual * product, axis=1)), "snp"
    )


def local(beta_hat, ld_band, band_start, heritability, genotypes):
    ridge_shift = M_GENOME / N_GWAS / heritability
    weights = jnp.zeros_like(beta_hat)
    residual = beta_hat
    product = apply_operator(residual, ld_band, band_start, ridge_shift)
    norm_now, mixed = paired_sums(residual, product)
    step_size = norm_now / mixed
    direction = residual
    along = product
    for turn_index in range(ITERS):
        weights = weights + step_size[:, None] * direction
        residual = residual - step_size[:, None] * along
        if turn_index + 1 < ITERS:
            product = apply_operator(residual, ld_band, band_start, ridge_shift)
            norm_next, mixed = paired_sums(residual, product)
            ratio_new = norm_next / norm_now
            step_size = norm_next / (mixed - ratio_new * norm_next / step_size)
            direction = residual + ratio_new[:, None] * direction
            along = product + ratio_new[:, None] * along
            norm_now = norm_next
    rounded = weights.astype(jnp.bfloat16)
    partial_scores = lax.dot_general(
        lax.all_gather(rounded, "ind", axis=0, tiled=True),
        genotypes,
        (((1,), (1,)), ((), ())),
        preferred_element_type=jnp.float32,
    )
    complete = lax.psum(partial_scores, "snp")
    count = complete.shape[1] * lax.axis_size("ind")
    summed = lax.psum(jnp.sum(complete, axis=1), "ind")
    average = summed / count
    centred = complete - average[:, None]
    variance = lax.psum(jnp.sum(centred * centred, axis=1), "ind") / count
    share_cols = complete.shape[1] // lax.axis_size("snp")
    own_part = lax.dynamic_slice_in_dim(centred, lax.axis_index("snp") * share_cols, share_cols, 1)
    scores = own_part * lax.rsqrt(variance + 1e-05)[:, None]
    return (weights, scores)


def solution(mesh):
    placed = (P("ind", "snp"), P("snp", None), P("snp"), P("ind"), P("ind", "snp"))
    return jax.shard_map(
        local,
        mesh=mesh,
        in_specs=placed,
        out_specs=(P("ind", "snp"), P(None, ("ind", "snp"))),
        check_vma=False,
    )
```

profile of v0, /device:TPU:0, one launch (start us, length us, event | category | flops | bytes accessed | tf_op | source)
XLA Modules:
  0.0 196.7 jit_solution(16912710394377717429)
XLA Ops:
  7.2 1.0 fusion.5
  8.2 4.9 %collective-permute-start = (f32[16,896]{1,0:T(8,128)S(1)}, f32[16,896]{1,0:T(8,128)S(1)}, u32[]{:S(2)}, u32[]{:S(2)}) collective-permute-start(f32[16,896]{1,0:T(8,128)S(1)} %get-tuple-element.50), channel_id=1, source_target_pairs={{0,4},{4,8},{8,12},{12,16},{16,20},{20,24},{24,28},{1,5},{5,9},{9,... | collective-permute-start | bytes 172040 | tf_op jit(solution)/shard_map/ppermute | solution.py:17
  13.1 1.3 collective-permute-start.1
  15.8 3.4 %collective-permute-done.1 = f32[16,896]{1,0:T(8,128)S(1)} collective-permute-done((f32[16,896]{1,0:T(8,128)S(1)}, f32[16,896]{1,0:T(8,128)S(1)}, u32[]{:S(2)}, u32[]{:S(2)}) %collective-permute-start.1) | collective-permute-done | bytes 57376 | tf_op jit(solution)/shard_map/ppermute | solution.py:20
  19.2 0.9 pad_maximum_fusion
  20.1 10.6 %while.2 = (s32[]{:T(128)}, f32[16,2816]{1,0:T(8,128)S(1)}, s32[8,2]{0,1:T(2,128)S(1)}, f32[8,16,1024]{2,1,0:T(8,128)S(1)}, s32[]{:T(128)}) while((s32[]{:T(128)}, f32[16,2816]{1,0:T(8,128)S(1)}, s32[8,2]{0,1:T(2,128)S(1)}, f32[8,16,1024]{2,1,0:T(8,128)S(1)}, s32[]{:T(128)}) %tuple.38), condition=%wide.while_cond, body=%wide.while_body.sunk | while | flops 2 | bytes 131169 | solution.py:31
  20.7 0.7 bitcast_dynamic-update-slice_fusion.4
  22.0 0.7 bitcast_dynamic-update-slice_fusion.4
  23.4 0.7 bitcast_dynamic-update-slice_fusion.4
  24.7 0.7 bitcast_dynamic-update-slice_fusion.4
  26.0 0.7 bitcast_dynamic-update-slice_fusion.4
  27.3 0.7 bitcast_dynamic-update-slice_fusion.4
  28.7 0.7 bitcast_dynamic-update-slice_fusion.4
  30.0 0.7 bitcast_dynamic-update-slice_fusion.4
  30.7 5.3 %convolution_bitcast_fusion.1 = f32[8,2,8,128]{3,2,1,0:T(8,128)S(1)} fusion(f32[8,16,1024]{2,1,0:T(8,128)S(1)} %get-tuple-element.9, f32[8,128,1024]{2,1,0:T(8,128)} %bitcast.41), kind=kOutput, calls=%fused_computation.5 | convolution fusion | flops 201326592 | bytes 4784128 | tf_op jit(solution)/shard_map/btk,brk->tbr/dot_general | solution.py:35
  36.2 19.8 %all-reduce.2 = (f32[16]{0:T(128)S(1)}, f32[16]{0:T(128)S(1)}) all-reduce(f32[16]{0:T(128)S(1)} %get-tuple-element.21, f32[16]{0:T(128)S(1)} %get-tuple-element.20), channel_id=1, replica_groups=mesh['snp'=8,'ind'=4] {'snp'}, use_global_device_ids=true, to_apply=%region_1.0 | all-reduce | flops 32 | bytes 256 | tf_op jit(solution)/shard_map/psum | solution.py:40
  56.2 1.6 collective-permute-start.2
  57.8 1.3 collective-permute-start.3
  59.6 4.3 %collective-permute-done.3 = f32[16,896]{1,0:T(8,128)S(1)} collective-permute-done((f32[16,896]{1,0:T(8,128)S(1)}, f32[16,896]{1,0:T(8,128)S(1)}, u32[]{:S(2)}, u32[]{:S(2)}) %collective-permute-start.3) | collective-permute-done | bytes 57376 | tf_op jit(solution)/shard_map/ppermute | solution.py:20
  63.9 10.6 %while.3 = (s32[]{:T(128)}, f32[16,2816]{1,0:T(8,128)S(1)}, s32[8,2]{0,1:T(2,128)S(1)}, f32[8,16,1024]{2,1,0:T(8,128)S(1)}, s32[]{:T(128)}) while((s32[]{:T(128)}, f32[16,2816]{1,0:T(8,128)S(1)}, s32[8,2]{0,1:T(2,128)S(1)}, f32[8,16,1024]{2,1,0:T(8,128)S(1)}, s32[]{:T(128)}) %tuple.46), condition=%wide.while_cond.1, body=%wide.while_body.1.sunk | while | flops 2 | bytes 131169 | solution.py:31
  64.5 0.7 bitcast_dynamic-update-slice_fusion.5
  65.8 0.7 bitcast_dynamic-update-slice_fusion.5
  72.5 0.7 bitcast_dynamic-update-slice_fusion.5
  74.5 5.3 %convolution_bitcast_fusion = f32[8,2,8,128]{3,2,1,0:T(8,128)S(1)} fusion(f32[8,16,1024]{2,1,0:T(8,128)S(1)} %get-tuple-element.17, f32[8,128,1024]{2,1,0:T(8,128)} %bitcast.42), kind=kOutput, calls=%fused_computation.4 | convolution fusion | flops 201326592 | bytes 4784128 | tf_op jit(solution)/shard_map/btk,brk->tbr/dot_general | solution.py:35
  80.0 18.6 %all-reduce.1 = (f32[16]{0:T(128)S(1)}, f32[16]{0:T(128)S(1)}) all-reduce(f32[16]{0:T(128)S(1)} %get-tuple-element.19, f32[16]{0:T(128)S(1)} %get-tuple-element.18), channel_id=1, replica_groups=mesh['snp'=8,'ind'=4] {'snp'}, use_global_device_ids=true, to_apply=%region_5.0 | all-reduce | flops 32 | bytes 256 | tf_op jit(solution)/shard_map/psum | solution.py:40
  99.3 5.4 %all_gather.3 = bf16[64,1024]{1,0:T(8,128)(2,1)S(1)} all-gather(bf16[16,1024]{1,0:T(8,128)(2,1)S(1)} %get-tuple-element.44), channel_id=1, replica_groups=mesh['snp'=8,'ind'=4] {'ind'}, dimensions={0}, use_global_device_ids=true | all-gather | bytes 163840 | tf_op jit(solution)/shard_map/all_gather | solution.py:67
  104.7 1.5 fusion.6
  106.2 68.5 %all-reduce.5.cloned.1.call-done = f32[64,1024]{1,0:T(8,128)} async-done(((f32[64,1024]{1,0:T(8,128)}), f32[64,1024]{1,0:T(8,128)}) %all-reduce.5.cloned.1.call-update) | async-done | bytes 262160 | tf_op jit(solution)/shard_map/psum | solution.py:72
  174.7 1.1 reduce_sum.58
  175.8 5.7 %psum.54 = f32[64]{0:T(128)S(1)} all-reduce(f32[64]{0:T(128)S(1)} %reduce_sum.58), channel_id=1, replica_groups=mesh['snp'=8,'ind'=4] {'ind'}, use_global_device_ids=true, to_apply=%region_10.0 | all-reduce | flops 64 | bytes 512 | tf_op jit(solution)/shard_map/psum | solution.py:74
  181.4 1.1 multiply_reduce_fusion
  182.6 6.6 %psum.55 = f32[64]{0:T(128)S(1)} all-reduce(f32[64]{0:T(128)S(1)} %get-tuple-element.42), channel_id=1, replica_groups=mesh['snp'=8,'ind'=4] {'ind'}, use_global_device_ids=true, to_apply=%region_12.0 | all-reduce | flops 64 | bytes 512 | tf_op jit(solution)/shard_map/psum | solution.py:77
  (61 shorter events, 17.1 us)
Async XLA Ops:
  7.2 97.5 %copy-start = (bf16[1024,1024]{1,0:T(8,128)(2,1)S(1)}, bf16[1024,1024]{1,0:T(8,128)(2,1)}, u32[]{:S(2)}) copy-start(bf16[1024,1024]{1,0:T(8,128)(2,1)} %param.9) | copy-start | bytes 6291460
  7.2 28.8 %copy-start.1 = (f32[16,1024]{1,0:T(8,128)S(1)}, f32[16,1024]{1,0:T(8,128)}, u32[]{:S(2)}) copy-start(f32[16,1024]{1,0:T(8,128)} %param.5) | copy-start | bytes 196612
  7.2 167.5 %all-reduce.5.cloned.1.call-start = ((), (), s32[]{:S(2)}) async-start(), calls=%async_computation | async-start | bytes 524288 | tf_op jit(solution)/shard_map/psum | solution.py:72
  8.2 7.5 %collective-permute-start = (f32[16,896]{1,0:T(8,128)S(1)}, f32[16,896]{1,0:T(8,128)S(1)}, u32[]{:S(2)}, u32[]{:S(2)}) collective-permute-start(f32[16,896]{1,0:T(8,128)S(1)} %get-tuple-element.50), channel_id=1, source_target_pairs={{0,4},{4,8},{8,12},{12,16},{16,20},{20,24},{24,28},{1,5},{5,9},{9,... | collective-permute-start | bytes 172040 | tf_op jit(solution)/shard_map/ppermute | solution.py:17
  13.1 6.1 %collective-permute-start.1 = (f32[16,896]{1,0:T(8,128)S(1)}, f32[16,896]{1,0:T(8,128)S(1)}, u32[]{:S(2)}, u32[]{:S(2)}) collective-permute-start(f32[16,896]{1,0:T(8,128)S(1)} %get-tuple-element.51), channel_id=1, source_target_pairs={{4,0},{8,4},{12,8},{16,12},{20,16},{24,20},{28,24},{5,1},{9,5},{13... | collective-permute-start | bytes 172040 | tf_op jit(solution)/shard_map/ppermute | solution.py:20
  56.2 3.4 %collective-permute-start.2 = (f32[16,896]{1,0:T(8,128)S(1)}, f32[16,896]{1,0:T(8,128)S(1)}, u32[]{:S(2)}, u32[]{:S(2)}) collective-permute-start(f32[16,896]{1,0:T(8,128)S(1)} %get-tuple-element.48), channel_id=1, source_target_pairs={{0,4},{4,8},{8,12},{12,16},{16,20},{20,24},{24,28},{1,5},{5,9},{9,... | collective-permute-start | bytes 172040 | tf_op jit(solution)/shard_map/ppermute | solution.py:17
  57.8 6.1 %collective-permute-start.3 = (f32[16,896]{1,0:T(8,128)S(1)}, f32[16,896]{1,0:T(8,128)S(1)}, u32[]{:S(2)}, u32[]{:S(2)}) collective-permute-start(f32[16,896]{1,0:T(8,128)S(1)} %get-tuple-element.49), channel_id=1, source_target_pairs={{4,0},{8,4},{12,8},{16,12},{20,16},{24,20},{28,24},{5,1},{9,5},{13... | collective-permute-start | bytes 172040 | tf_op jit(solution)/shard_map/ppermute | solution.py:20
Sparse Core Ops, SparseCore 0:
  106.3 68.3 all-reduce.4
where the time goes:
time: 197 us
  waiting for transfers between devices  76.7 us (39%)
  blocking collectives  56.1 us (28%)
  local copies, waits for them, and re-layouts  22.3 us (11%)
  between operations  14.1 us (7%)
  matrix products  12 us (6%)
  starting transfers between devices  9.11 us (5%)
  other arithmetic  6.34 us (3%)
    psum x1, waiting for transfers between devices, local(): complete = lax.psum(partial_scores, 'snp')  68.5 us
    psum x2, blocking collectives, paired_sums(): lax.psum((jnp.sum(residual * residual, axis=1), jnp.sum(residual * produc...  38.4 us
    gather x48, local copies, waits for them, and re-layouts  21.1 us
    dot_general x2, matrix products, apply_operator(): jnp.einsum('btk,brk->tbr', windows, blocks, precision=lax.Precision.HIGHEST)  10.6 us
    ppermute x2, waiting for transfers between devices, padded_2(): lax.ppermute(lax.slice_in_dim(block, 0, width, axis=dim), axis, backward)  7.69 us
    psum x1, blocking collectives, local(): variance = lax.psum(jnp.sum(centred * centred, axis=1), 'ind') / count  6.6 us
    ppermute x2, starting transfers between devices, padded_2(): lax.ppermute(lax.slice_in_dim(block, block.shape[dim] - width, None, axis...  6.49 us
    psum x1, blocking collectives, local(): summed = lax.psum(jnp.sum(complete, axis=1), 'ind')  5.67 us
  transfers between devices with their start and end apart: 5, of which 4 were waited for; matrix products, arithmetic and copies ran while one was open for 1% of the time, Pallas kernels for 0%

commit v1 on v0

--- a/solution.py
+++ b/solution.py
@@ -69,7 +69,7 @@
         (((1,), (1,)), ((), ())),
         preferred_element_type=jnp.float32,
     )
-    complete = lax.psum(partial_scores, "snp")
+    complete = jnp.sum(lax.all_gather(partial_scores, "snp"), axis=0)
     count = complete.shape[1] * lax.axis_size("ind")
     summed = lax.psum(jnp.sum(complete, axis=1), "ind")
     average = summed / count

time: 197 us -> 177 us (0.90)
  waiting for transfers between devices: 76.7 us -> 54.7 us
    psum x1 -> x0, waiting for transfers between devices: 68.5 us -> none  [local(): complete = lax.psum(partial_scores, 'snp')]
    all_gather x0 -> x1, waiting for transfers between devices: none -> 46.5 us  [local(): complete = jnp.sum(lax.all_gather(partial_scores, 'snp'), axis=0)]
where the time goes in v1:
time: 177 us; the launch traced here: 176 us
  blocking collectives  56.1 us (32%)
  waiting for transfers between devices  54.7 us (31%)
  local copies, waits for them, and re-layouts  22.3 us (13%)
  between operations  14.1 us (8%)
  matrix products  12.1 us (7%)
  starting transfers between devices  9.11 us (5%)
  other arithmetic  7.86 us (4%)
    all_gather x1, waiting for transfers between devices, local(): complete = jnp.sum(lax.all_gather(partial_scores, 'snp'), axis=0)  46.5 us
    psum x2, blocking collectives, paired_sums(): lax.psum((jnp.sum(residual * residual, axis=1), jnp.sum(residual * produc...  38.4 us
    gather x48, local copies, waits for them, and re-layouts  21.1 us
    dot_general x2, matrix products, apply_operator(): jnp.einsum('btk,brk->tbr', windows, blocks, precision=lax.Precision.HIGHEST)  10.6 us
    ppermute x2, waiting for transfers between devices, padded_2(): lax.ppermute(lax.slice_in_dim(block, 0, width, axis=dim), axis, backward)  7.69 us
    psum x1, blocking collectives, local(): variance = lax.psum(jnp.sum(centred * centred, axis=1), 'ind') / count  6.59 us
    ppermute x2, starting transfers between devices, padded_2(): lax.ppermute(lax.slice_in_dim(block, block.shape[dim] - width, None, axis...  6.49 us
    psum x1, blocking collectives, local(): summed = lax.psum(jnp.sum(complete, axis=1), 'ind')  5.66 us
  transfers between devices with their start and end apart: 5, of which 4 were waited for; matrix products, arithmetic and copies ran while one was open for 1% of the time, Pallas kernels for 0%

profile of v1, /device:TPU:0, one launch (start us, length us, event | category | flops | bytes accessed | tf_op | source)
XLA Modules:
  0.0 176.4 jit_solution(5783423522611129500)
XLA Ops:
  7.2 1.0 fusion.5
  8.2 4.9 %collective-permute-start = (f32[16,896]{1,0:T(8,128)S(1)}, f32[16,896]{1,0:T(8,128)S(1)}, u32[]{:S(2)}, u32[]{:S(2)}) collective-permute-start(f32[16,896]{1,0:T(8,128)S(1)} %get-tuple-element.50), channel_id=1, source_target_pairs={{0,4},{4,8},{8,12},{12,16},{16,20},{20,24},{24,28},{1,5},{5,9},{9,... | collective-permute-start | bytes 172040 | tf_op jit(solution)/shard_map/ppermute | solution.py:17
  13.1 1.3 collective-permute-start.1
  15.8 3.4 %collective-permute-done.1 = f32[16,896]{1,0:T(8,128)S(1)} collective-permute-done((f32[16,896]{1,0:T(8,128)S(1)}, f32[16,896]{1,0:T(8,128)S(1)}, u32[]{:S(2)}, u32[]{:S(2)}) %collective-permute-start.1) | collective-permute-done | bytes 57376 | tf_op jit(solution)/shard_map/ppermute | solution.py:20
  19.2 0.9 pad_maximum_fusion
  20.1 10.6 %while.2 = (s32[]{:T(128)}, f32[16,2816]{1,0:T(8,128)S(1)}, s32[8,2]{0,1:T(2,128)S(1)}, f32[8,16,1024]{2,1,0:T(8,128)S(1)}, s32[]{:T(128)}) while((s32[]{:T(128)}, f32[16,2816]{1,0:T(8,128)S(1)}, s32[8,2]{0,1:T(2,128)S(1)}, f32[8,16,1024]{2,1,0:T(8,128)S(1)}, s32[]{:T(128)}) %tuple.38), condition=%wide.while_cond, body=%wide.while_body.sunk | while | flops 2 | bytes 131177 | solution.py:31
  20.7 0.7 bitcast_dynamic-update-slice_fusion.4
  22.0 0.7 bitcast_dynamic-update-slice_fusion.4
  23.4 0.7 bitcast_dynamic-update-slice_fusion.4
  24.7 0.7 bitcast_dynamic-update-slice_fusion.4
  26.0 0.7 bitcast_dynamic-update-slice_fusion.4
  27.3 0.7 bitcast_dynamic-update-slice_fusion.4
  28.7 0.7 bitcast_dynamic-update-slice_fusion.4
  30.0 0.7 bitcast_dynamic-update-slice_fusion.4
  30.7 5.3 %convolution_bitcast_fusion.1 = f32[8,2,8,128]{3,2,1,0:T(8,128)S(1)} fusion(f32[8,16,1024]{2,1,0:T(8,128)S(1)} %get-tuple-element.9, f32[8,128,1024]{2,1,0:T(8,128)} %bitcast.42), kind=kOutput, calls=%fused_computation.5 | convolution fusion | flops 201326592 | bytes 4784128 | tf_op jit(solution)/shard_map/btk,brk->tbr/dot_general | solution.py:35
  36.2 19.8 %all-reduce.2 = (f32[16]{0:T(128)S(1)}, f32[16]{0:T(128)S(1)}) all-reduce(f32[16]{0:T(128)S(1)} %get-tuple-element.21, f32[16]{0:T(128)S(1)} %get-tuple-element.20), channel_id=1, replica_groups=mesh['snp'=8,'ind'=4] {'snp'}, use_global_device_ids=true, to_apply=%region_1.0 | all-reduce | flops 32 | bytes 256 | tf_op jit(solution)/shard_map/psum | solution.py:40
  56.2 1.6 collective-permute-start.2
  57.8 1.3 collective-permute-start.3
  59.6 4.3 %collective-permute-done.3 = f32[16,896]{1,0:T(8,128)S(1)} collective-permute-done((f32[16,896]{1,0:T(8,128)S(1)}, f32[16,896]{1,0:T(8,128)S(1)}, u32[]{:S(2)}, u32[]{:S(2)}) %collective-permute-start.3) | collective-permute-done | bytes 57376 | tf_op jit(solution)/shard_map/ppermute | solution.py:20
  63.9 10.6 %while.3 = (s32[]{:T(128)}, f32[16,2816]{1,0:T(8,128)S(1)}, s32[8,2]{0,1:T(2,128)S(1)}, f32[8,16,1024]{2,1,0:T(8,128)S(1)}, s32[]{:T(128)}) while((s32[]{:T(128)}, f32[16,2816]{1,0:T(8,128)S(1)}, s32[8,2]{0,1:T(2,128)S(1)}, f32[8,16,1024]{2,1,0:T(8,128)S(1)}, s32[]{:T(128)}) %tuple.46), condition=%wide.while_cond.1, body=%wide.while_body.1.sunk | while | flops 2 | bytes 131177 | solution.py:31
  64.5 0.7 bitcast_dynamic-update-slice_fusion.5
  65.8 0.7 bitcast_dynamic-update-slice_fusion.5
  72.5 0.7 bitcast_dynamic-update-slice_fusion.5
  74.5 5.3 %convolution_bitcast_fusion = f32[8,2,8,128]{3,2,1,0:T(8,128)S(1)} fusion(f32[8,16,1024]{2,1,0:T(8,128)S(1)} %get-tuple-element.17, f32[8,128,1024]{2,1,0:T(8,128)} %bitcast.43), kind=kOutput, calls=%fused_computation.4 | convolution fusion | flops 201326592 | bytes 4784128 | tf_op jit(solution)/shard_map/btk,brk->tbr/dot_general | solution.py:35
  80.0 18.6 %all-reduce.1 = (f32[16]{0:T(128)S(1)}, f32[16]{0:T(128)S(1)}) all-reduce(f32[16]{0:T(128)S(1)} %get-tuple-element.19, f32[16]{0:T(128)S(1)} %get-tuple-element.18), channel_id=1, replica_groups=mesh['snp'=8,'ind'=4] {'snp'}, use_global_device_ids=true, to_apply=%region_5.0 | all-reduce | flops 32 | bytes 256 | tf_op jit(solution)/shard_map/psum | solution.py:40
  99.3 5.4 %all_gather.9 = bf16[64,1024]{1,0:T(8,128)(2,1)S(1)} all-gather(bf16[16,1024]{1,0:T(8,128)(2,1)S(1)} %get-tuple-element.44), channel_id=1, replica_groups=mesh['snp'=8,'ind'=4] {'ind'}, dimensions={0}, use_global_device_ids=true | all-gather | bytes 163840 | tf_op jit(solution)/shard_map/all_gather | solution.py:67
  104.7 1.5 fusion.6
  106.2 46.5 %all-gather.3.cloned.1.call-done = f32[512,1024]{1,0:T(8,128)} async-done(((f32[64,1024]{1,0:T(8,128)}), f32[512,1024]{1,0:T(8,128)}) %all-gather.3.cloned.1.call-update) | async-done | bytes 2097168 | tf_op jit(solution)/shard_map/all_gather | solution.py:72
  152.7 1.8 %reduce.1 = f32[512]{0:T(512)S(1)} reduce(f32[512,1024]{1,0:T(8,128)} %all-gather.3.cloned.1.call-done, f32[]{:T(128)} %constant.11.clone.1), dimensions={1}, to_apply=%region_9.0 | reduce | flops 523776 | bytes 2099204 | tf_op jit(solution)/shard_map/reduce_sum | solution.py:74
  154.6 5.7 %psum.46 = f32[64]{0:T(128)S(1)} all-reduce(f32[64]{0:T(128)S(1)} %reduce_sum.68), channel_id=1, replica_groups=mesh['snp'=8,'ind'=4] {'ind'}, use_global_device_ids=true, to_apply=%region_10.0 | all-reduce | flops 64 | bytes 512 | tf_op jit(solution)/shard_map/psum | solution.py:74
  160.3 1.7 reduce_sum.67
  162.2 6.6 %psum.47 = f32[64]{0:T(128)S(1)} all-reduce(f32[64]{0:T(128)S(1)} %get-tuple-element.42), channel_id=1, replica_groups=mesh['snp'=8,'ind'=4] {'ind'}, use_global_device_ids=true, to_apply=%region_12.0 | all-reduce | flops 64 | bytes 512 | tf_op jit(solution)/shard_map/psum | solution.py:77
  (64 shorter events, 17.4 us)
Async XLA Ops:
  7.2 97.5 %copy-start = (bf16[1024,1024]{1,0:T(8,128)(2,1)S(1)}, bf16[1024,1024]{1,0:T(8,128)(2,1)}, u32[]{:S(2)}) copy-start(bf16[1024,1024]{1,0:T(8,128)(2,1)} %param.9) | copy-start | bytes 6291460
  7.2 28.8 %copy-start.1 = (f32[16,1024]{1,0:T(8,128)S(1)}, f32[16,1024]{1,0:T(8,128)}, u32[]{:S(2)}) copy-start(f32[16,1024]{1,0:T(8,128)} %param.5) | copy-start | bytes 196612
  7.2 145.5 %all-gather.3.cloned.1.call-start = ((), (), s32[]{:S(2)}) async-start(), calls=%async_computation | async-start | bytes 2359296 | tf_op jit(solution)/shard_map/all_gather | solution.py:72
  8.2 7.5 %collective-permute-start = (f32[16,896]{1,0:T(8,128)S(1)}, f32[16,896]{1,0:T(8,128)S(1)}, u32[]{:S(2)}, u32[]{:S(2)}) collective-permute-start(f32[16,896]{1,0:T(8,128)S(1)} %get-tuple-element.50), channel_id=1, source_target_pairs={{0,4},{4,8},{8,12},{12,16},{16,20},{20,24},{24,28},{1,5},{5,9},{9,... | collective-permute-start | bytes 172040 | tf_op jit(solution)/shard_map/ppermute | solution.py:17
  13.1 6.1 %collective-permute-start.1 = (f32[16,896]{1,0:T(8,128)S(1)}, f32[16,896]{1,0:T(8,128)S(1)}, u32[]{:S(2)}, u32[]{:S(2)}) collective-permute-start(f32[16,896]{1,0:T(8,128)S(1)} %get-tuple-element.51), channel_id=1, source_target_pairs={{4,0},{8,4},{12,8},{16,12},{20,16},{24,20},{28,24},{5,1},{9,5},{13... | collective-permute-start | bytes 172040 | tf_op jit(solution)/shard_map/ppermute | solution.py:20
  56.2 3.4 %collective-permute-start.2 = (f32[16,896]{1,0:T(8,128)S(1)}, f32[16,896]{1,0:T(8,128)S(1)}, u32[]{:S(2)}, u32[]{:S(2)}) collective-permute-start(f32[16,896]{1,0:T(8,128)S(1)} %get-tuple-element.48), channel_id=1, source_target_pairs={{0,4},{4,8},{8,12},{12,16},{16,20},{20,24},{24,28},{1,5},{5,9},{9,... | collective-permute-start | bytes 172040 | tf_op jit(solution)/shard_map/ppermute | solution.py:17
  57.8 6.1 %collective-permute-start.3 = (f32[16,896]{1,0:T(8,128)S(1)}, f32[16,896]{1,0:T(8,128)S(1)}, u32[]{:S(2)}, u32[]{:S(2)}) collective-permute-start(f32[16,896]{1,0:T(8,128)S(1)} %get-tuple-element.49), channel_id=1, source_target_pairs={{4,0},{8,4},{12,8},{16,12},{20,16},{24,20},{28,24},{5,1},{9,5},{13... | collective-permute-start | bytes 172040 | tf_op jit(solution)/shard_map/ppermute | solution.py:20
Sparse Core Ops, SparseCore 0:
  106.3 46.3 all-gather.2
